TPU v7x, 512 devices: a whole 4x8x8 slice. The times are simulated.
512 devices in a mesh: ctx: 32 (over y_lo, z, core), tp: 16 (over x, y_hi).
Axes of the slice: x: 4, y: 8 (y_hi: 4, y_lo: 2; y = y_hi * 2 + y_lo), z: 8, core: 2. Of those that a mesh axis runs over, the one named last changes fastest.
Arguments:
- query: bfloat16 [8192, 4096], P('ctx', 'tp'), may hold values from 0.049804688 to 2
- key_feat: bfloat16 [8192, 4096], P('ctx', 'tp'), may hold values from 0.049804688 to 2
- value: bfloat16 [8192, 4096], P('ctx', 'tp'), may hold values from -36 to 36
- grad_out: bfloat16 [8192, 4096], P('ctx', 'tp'), may hold values from -6 to 6
- w_out: bfloat16 [4096, 4096], P('tp', 'ctx'), may hold values from -0.09375 to 0.09375
Outputs:
- grad_query: bfloat16 [8192, 4096], P('ctx', 'tp')
- grad_key: bfloat16 [8192, 4096], P('ctx', 'tp')
- grad_value: bfloat16 [8192, 4096], P('ctx', 'tp')
All inputs are finite; a program needn't handle non-finite values.
Results may differ from a plain program's by a relative error of at most 0.0059.
Values may be sent and summed in bfloat16 or wider, within the bound.
No kernel may reach another device: no remote copies, remote signals or barrier semaphores. Data moves between devices by JAX's collectives and lax.ppermute only.
A program may use at most 64 MiB of HBM per device.

v0:
```python
import jax
import jax.numpy as jnp
from jax import lax
from jax.sharding import PartitionSpec as P

E = 128
epsilon = 1e-06
highest = lax.Precision.HIGHEST


def prefix(value, axis, join, neutral, backward):
    count, mine = (lax.axis_size(axis), lax.axis_index(axis))
    pieces = lax.all_gather(value, axis)
    if backward:
        pieces = pieces[::-1]
        mine = count - 1 - mine
    subtotal = jnp.full_like(value, 0) + jnp.asarray(neutral, value.dtype)

    def lap(position, subtotal):
        longer = join(subtotal, pieces[position])
        return jnp.where(position < mine, longer, subtotal)

    return lax.fori_loop(0, count - 1, lap, subtotal)


def add_states(earlier, later):
    return earlier + later


def local(query, key_feat, value, grad_out, w_out):
    tok_rows = query.shape[0]
    feat_width = query.shape[1]
    head_count = feat_width // E
    full_rows = lax.all_gather(grad_out, "tp", axis=1, tiled=True)
    grad_z = lax.dot_general(
        full_rows,
        lax.all_gather(w_out, "ctx", axis=1, tiled=True),
        (((1,), (1,)), ((), ())),
        preferred_element_type=jnp.float32,
    )
    query_heads = query.reshape(tok_rows, head_count, E)
    key_heads = key_feat.reshape(tok_rows, head_count, E)
    value_heads = value.reshape(tok_rows, head_count, E)
    gradz_heads = grad_z.reshape(tok_rows, head_count, E)
    query_wide = query_heads.astype(jnp.float32)
    key_wide = key_heads.astype(jnp.float32)
    value_wide = value_heads.astype(jnp.float32)
    causal = (
        lax.broadcasted_iota(jnp.int32, (tok_rows, tok_rows), 0)
        >= lax.broadcasted_iota(jnp.int32, (tok_rows, tok_rows), 1)
    )[None]
    scores = jnp.einsum("thd,shd->hts", query_heads, key_heads, preferred_element_type=jnp.float32)
    weights = jnp.where(causal, scores, 0.0)
    local_state = jnp.einsum(
        "shd,she->hde", key_heads, value_heads, preferred_element_type=jnp.float32
    )
    empty_state = jnp.zeros_like(local_state)
    state_in = prefix(local_state, "ctx", add_states, empty_state, False)
    attended = jnp.einsum("hts,she->the", weights, value_wide, precision=highest)
    attended = attended + jnp.einsum("thd,hde->the", query_wide, state_in, precision=highest)
    inv_rms = lax.rsqrt(jnp.mean(attended * attended, axis=-1, keepdims=True) + epsilon)
    normed = attended * inv_rms
    grad_att = (
        inv_rms * (gradz_heads - normed * jnp.mean(gradz_heads * normed, axis=-1, keepdims=True))
    ).astype(jnp.bfloat16)
    grad_wide = grad_att.astype(jnp.float32)
    grad_weights = jnp.where(
        causal,
        jnp.einsum("the,she->hts", grad_att, value_heads, preferred_element_type=jnp.float32),
        0.0,
    )
    grad_query = jnp.einsum("hts,shd->thd", grad_weights, key_wide, precision=highest)
    grad_query = grad_query + jnp.einsum("the,hde->thd", grad_wide, state_in, precision=highest)
    local_adjoint = jnp.einsum(
        "thd,the->hde", query_heads, grad_att, preferred_element_type=jnp.float32
    )
    adjoint = prefix(local_adjoint, "ctx", add_states, empty_state, True)
    grad_key = jnp.einsum("hts,thd->shd", grad_weights, query_wide, precision=highest)
    grad_key = grad_key + jnp.einsum("she,hde->shd", value_wide, adjoint, precision=highest)
    grad_value = jnp.einsum("hts,the->she", weights, grad_wide, precision=highest)
    grad_value = grad_value + jnp.einsum("shd,hde->she", key_wide, adjoint, precision=highest)
    return (
        grad_query.reshape(tok_rows, feat_width).astype(jnp.bfloat16),
        grad_key.reshape(tok_rows, feat_width).astype(jnp.bfloat16),
        grad_value.reshape(tok_rows, feat_width).astype(jnp.bfloat16),
    )


def solution(mesh):
    return jax.shard_map(
        local,
        mesh=mesh,
        in_specs=(P("ctx", "tp"), P("ctx", "tp"), P("ctx", "tp"), P("ctx", "tp"), P("tp", "ctx")),
        out_specs=(P("ctx", "tp"), P("ctx", "tp"), P("ctx", "tp")),
        check_vma=False,
    )
```

profile of v0, /device:TPU:1, one launch (start us, length us, event | category | flops | bytes accessed | tf_op | source)
XLA Modules:
  0.0 341.3 jit_solution(11616398118935155709)
XLA Ops:
  7.2 1.1 copy.95
  10.8 1.2 convolution_select_fusion.1
  12.0 74.3 %all-gather.11.cloned.1.call-done = f32[64,128,128]{2,1,0:T(8,128)} async-done(((f32[2,128,128]{2,1,0:T(8,128)}), f32[64,128,128]{2,1,0:T(8,128)}) %all-gather.11.cloned.1.call-update) | async-done | bytes 4194320 | tf_op jit(solution)/shard_map/all_gather | solution.py:13
  86.3 30.2 %while.28 = (s32[]{:T(128)}, f32[2,128,128]{2,1,0:T(8,128)S(1)}, s32[]{:T(128)}, f32[32,2,128,128]{3,2,1,0:T(8,128)}, s32[]{:T(128)}, /*index=5*/s32[]{:T(128)}) while((s32[]{:T(128)}, f32[2,128,128]{2,1,0:T(8,128)S(1)}, s32[]{:T(128)}, f32[32,2,128,128]{3,2,1,0:T(8,128)}, s32[]{:T(128)}, /*index=5*/s32[]{:T(128)}) %tuple.81), condition=%wide.region_1.2_spmd.clone, body=%wide.region_0.1_spmd.clone.sunk | while | flops 98308 | bytes 393317 | solution.py:23
  87.2 0.9 add_select_fusion.4
  88.2 0.9 add_select_fusion.4
  89.2 0.9 add_select_fusion.4
  90.2 0.9 add_select_fusion.4
  91.1 0.9 add_select_fusion.4
  92.1 0.9 add_select_fusion.4
  93.1 0.9 add_select_fusion.4
  94.1 0.9 add_select_fusion.4
  95.0 0.9 add_select_fusion.4
  96.0 0.9 add_select_fusion.4
  97.0 0.9 add_select_fusion.4
  98.0 0.9 add_select_fusion.4
  98.9 0.9 add_select_fusion.4
  99.9 0.9 add_select_fusion.4
  100.9 0.9 add_select_fusion.4
  101.8 0.9 add_select_fusion.4
  102.8 1.0 add_select_fusion.4
  103.8 1.0 add_select_fusion.4
  104.8 0.9 add_select_fusion.4
  105.7 0.9 add_select_fusion.4
  106.7 0.9 add_select_fusion.4
  107.7 0.9 add_select_fusion.4
  108.7 0.9 add_select_fusion.4
  109.6 1.0 add_select_fusion.4
  110.6 1.0 add_select_fusion.4
  111.6 0.9 add_select_fusion.4
  112.6 0.9 add_select_fusion.4
  113.5 0.9 add_select_fusion.4
  114.5 1.0 add_select_fusion.4
  115.5 0.9 add_select_fusion.4
  117.3 36.0 %all-gather.7.cloned.1.call-done = bf16[256,4096]{1,0:T(8,128)(2,1)} async-done(((bf16[256,256]{1,0:T(8,128)(2,1)}), bf16[256,4096]{1,0:T(8,128)(2,1)}) %all-gather.7.cloned.1.call-update) | async-done | bytes 2097168 | tf_op jit(solution)/shard_map/all_gather | solution.py:34
  153.3 72.8 %all-gather.9.cloned.1.call-done = bf16[256,4096]{1,0:T(8,128)(2,1)} async-done(((bf16[256,128]{1,0:T(8,128)(2,1)}), bf16[256,4096]{1,0:T(8,128)(2,1)}) %all-gather.9.cloned.1.call-update) | async-done | bytes 2097168 | tf_op jit(solution)/shard_map/all_gather | solution.py:37
  226.1 3.0 multiply_reduce_fusion
  232.2 65.2 %all-gather.13.cloned.1.call-done = f32[64,128,128]{2,1,0:T(8,128)} async-done(((f32[2,128,128]{2,1,0:T(8,128)}), f32[64,128,128]{2,1,0:T(8,128)}) %all-gather.13.cloned.1.call-update) | async-done | bytes 4194320 | tf_op jit(solution)/shard_map/all_gather | solution.py:13
  297.4 4.7 %rev.3 = f32[32,2,128,128]{3,2,1,0:T(8,128)} reverse(f32[32,2,128,128]{3,2,1,0:T(8,128)} %bitcast.117), dimensions={0} | reverse | bytes 8388608 | tf_op jit(solution)/shard_map/rev | solution.py:15
  302.1 30.2 %while.29 = (s32[]{:T(128)}, f32[2,128,128]{2,1,0:T(8,128)S(1)}, s32[]{:T(128)}, f32[32,2,128,128]{3,2,1,0:T(8,128)}, s32[]{:T(128)}, /*index=5*/s32[]{:T(128)}) while((s32[]{:T(128)}, f32[2,128,128]{2,1,0:T(8,128)S(1)}, s32[]{:T(128)}, f32[32,2,128,128]{3,2,1,0:T(8,128)}, s32[]{:T(128)}, /*index=5*/s32[]{:T(128)}) %tuple.70), condition=%wide.region_5.6_spmd.clone, body=%wide.region_4.5_spmd.clone.sunk | while | flops 98308 | bytes 393317 | solution.py:23
  302.1 1.0 add_select_fusion.5
  303.1 0.9 add_select_fusion.5
  304.1 0.9 add_select_fusion.5
  305.0 0.9 add_select_fusion.5
  306.0 0.9 add_select_fusion.5
  307.0 0.9 add_select_fusion.5
  307.9 0.9 add_select_fusion.5
  308.9 0.9 add_select_fusion.5
  (59 shorter events, 31.5 us)
Async XLA Ops:
  7.2 1.1 copy-start
  7.2 109.3 %copy-start.1 = (bf16[256,256]{1,0:T(8,128)(2,1)S(1)}, bf16[256,256]{1,0:T(8,128)(2,1)}, u32[]{:S(2)}) copy-start(bf16[256,256]{1,0:T(8,128)(2,1)} %param.9) | copy-start | bytes 393220
  7.2 79.1 %all-gather.11.cloned.1.call-start = ((), (), s32[]{:S(2)}) async-start(), calls=%async_computation.2 | async-start | bytes 4325376 | tf_op jit(solution)/shard_map/all_gather | solution.py:13
  9.2 144.1 %all-gather.7.cloned.1.call-start = ((), (), s32[]{:S(2)}) async-start(), calls=%async_computation | async-start | bytes 2228224 | tf_op jit(solution)/shard_map/all_gather | solution.py:34
  9.9 216.1 %all-gather.9.cloned.1.call-start = ((), (), s32[]{:S(2)}) async-start(), calls=%async_computation.1 | async-start | bytes 2162688 | tf_op jit(solution)/shard_map/all_gather | solution.py:37
  10.7 286.8 %all-gather.13.cloned.1.call-start = ((), (), s32[]{:S(2)}) async-start(), calls=%async_computation.3 | async-start | bytes 4325376 | tf_op jit(solution)/shard_map/all_gather | solution.py:13
  302.1 30.5 %copy-start.2 = (bf16[256,256]{1,0:T(8,128)(2,1)S(1)}, bf16[256,256]{1,0:T(8,128)(2,1)}, u32[]{:S(2)}) copy-start(bf16[256,256]{1,0:T(8,128)(2,1)} %param.10) | copy-start | bytes 393220
Sparse Core Ops, SparseCore 0:
  10.7 75.5 all-gather.10
  89.3 63.9 all-gather.6
  155.3 70.6 all-gather.8
  230.2 67.1 all-gather.12
where the time goes:
time: 343 us; the launch traced here: 341 us
  waiting for transfers between devices  250 us (73%)
  other arithmetic  59 us (17%)
  between operations  13.9 us (4%)
  local copies, waits for them, and re-layouts  8.78 us (3%)
  matrix products  8.2 us (2%)
    all_gather x2, waiting for transfers between devices, prefix(): pieces = lax.all_gather(value, axis)  140 us
    all_gather x1, waiting for transfers between devices, local(): lax.all_gather(w_out, 'ctx', axis=1, tiled=True)  72.8 us
    select_n x62, other arithmetic, lap(): return jnp.where(position < mine, longer, subtotal)  58.9 us
    all_gather x1, waiting for transfers between devices, local(): full_rows = lax.all_gather(grad_out, 'tp', axis=1, tiled=True)  36 us
  transfers between devices with their start and end apart: 4, of which 4 were waited for; matrix products, arithmetic and copies ran while one was open for 10% of the time, Pallas kernels for 0%

commit v1 on v0

--- a/solution.py
+++ b/solution.py
@@ -6,6 +6,13 @@
 E = 128
 epsilon = 1e-06
 highest = lax.Precision.HIGHEST
+
+
+def mix_paths(local_values):
+    local_now = jnp.stack([local_values for _ in range(lax.axis_size("tp"))], 0)
+    lower = lax.all_to_all(local_now, "tp", 0, 0)
+    local_next = jnp.concatenate(lower, 1)
+    return local_next
 
 
 def prefix(value, axis, join, neutral, backward):
@@ -31,7 +38,7 @@
     tok_rows = query.shape[0]
     feat_width = query.shape[1]
     head_count = feat_width // E
-    full_rows = lax.all_gather(grad_out, "tp", axis=1, tiled=True)
+    full_rows = mix_paths(grad_out)
     grad_z = lax.dot_general(
         full_rows,
         lax.all_gather(w_out, "ctx", axis=1, tiled=True),

time: 343 us -> 287 us (0.84)
  waiting for transfers between devices: 250 us -> 176 us
  starting transfers between devices: 0.16 us -> 10.5 us
  local copies, waits for them, and re-layouts: 8.78 us -> 17.2 us
    all_gather x2, waiting for transfers between devices: 140 us -> 72.6 us  [prefix(): pieces = lax.all_gather(value, axis)]
    all_to_all x0 -> x1, waiting for transfers between devices: none -> 64 us  [mix_paths(): lower = lax.all_to_all(local_now, 'tp', 0, 0)]
    all_gather x1 -> x0, waiting for transfers between devices: 36 us -> none  [local(): full_rows = lax.all_gather(grad_out, 'tp', axis=1, tiled=True)]
    all_gather x1, waiting for transfers between devices: 72.8 us -> 38.9 us  [local(): lax.all_gather(w_out, 'ctx', axis=1, tiled=True)]
    all_to_all x0 -> x1, starting transfers between devices: none -> 10.3 us  [mix_paths(): lower = lax.all_to_all(local_now, 'tp', 0, 0)]
    reshape x0 -> x2, local copies, waits for them, and re-layouts: none -> 5.43 us  [mix_paths(): local_next = jnp.concatenate(lower, 1)]
  transfers between devices with their start and end apart: 4 -> 4, of which waited for: 4 -> 4; matrix products, arithmetic and copies ran while one was open for 10% -> 14% of each run, Pallas kernels for 0% -> 0%
where the time goes in v1:
time: 287 us; the launch traced here: 286 us
  waiting for transfers between devices  176 us (61%)
  other arithmetic  59 us (21%)
  local copies, waits for them, and re-layouts  17.2 us (6%)
  between operations  13.9 us (5%)
  starting transfers between devices  10.5 us (4%)
  matrix products  7.42 us (3%)
    all_gather x2, waiting for transfers between devices, prefix(): pieces = lax.all_gather(value, axis)  72.6 us
    all_to_all x1, waiting for transfers between devices, mix_paths(): lower = lax.all_to_all(local_now, 'tp', 0, 0)  64 us
    select_n x62, other arithmetic, lap(): return jnp.where(position < mine, longer, subtotal)  58.9 us
    all_gather x1, waiting for transfers between devices, local(): lax.all_gather(w_out, 'ctx', axis=1, tiled=True)  38.9 us
    all_to_all x1, starting transfers between devices, mix_paths(): lower = lax.all_to_all(local_now, 'tp', 0, 0)  10.3 us
  transfers between devices with their start and end apart: 4, of which 4 were waited for; matrix products, arithmetic and copies ran while one was open for 14% of the time, Pallas kernels for 0%

profile of v1, /device:TPU:1, one launch (start us, length us, event | category | flops | bytes accessed | tf_op | source)
XLA Modules:
  0.0 285.6 jit_solution(11122565761470836422)
XLA Ops:
  7.2 1.0 copy.96
  9.1 2.5 stack.2
  11.6 10.3 %all-to-all-start = ((bf16[16,256,256]{2,1,0:T(8,128)(2,1)}), bf16[16,256,256]{2,1,0:T(8,128)(2,1)S(1)}, u32[]{:S(2)}, u32[]{:S(2)}) async-start(bf16[16,256,256]{2,1,0:T(8,128)(2,1)} %stack.2), calls=%async_computation | async-start | bytes 4194304 | tf_op jit(solution)/shard_map/all_to_all | solution.py:13
  23.7 64.0 %all-to-all-done = bf16[16,256,256]{2,1,0:T(8,128)(2,1)S(1)} async-done(((bf16[16,256,256]{2,1,0:T(8,128)(2,1)}), bf16[16,256,256]{2,1,0:T(8,128)(2,1)S(1)}, u32[]{:S(2)}, u32[]{:S(2)}) %all-to-all-start) | async-done | bytes 2097184 | tf_op jit(solution)/shard_map/all_to_all | solution.py:13
  87.6 2.5 copy.35
  90.2 2.9 %reshape.57 = bf16[256,4096,1]{1,0,2:T(8,128)(2,1)S(1)} reshape(bf16[256,16,256]{2,1,0:T(8,128)(2,1)} %copy.35) | data formatting | bytes 4194304 | tf_op jit(solution)/shard_map/reshape | solution.py:14
  93.1 8.1 %all-gather.8.cloned.1.call-done = f32[64,128,128]{2,1,0:T(8,128)} async-done(((f32[2,128,128]{2,1,0:T(8,128)}), f32[64,128,128]{2,1,0:T(8,128)}) %all-gather.8.cloned.1.call-update) | async-done | bytes 4194320 | tf_op jit(solution)/shard_map/all_gather | solution.py:20
  101.2 30.2 %while.28 = (s32[]{:T(128)}, f32[2,128,128]{2,1,0:T(8,128)S(1)}, s32[]{:T(128)}, f32[32,2,128,128]{3,2,1,0:T(8,128)}, s32[]{:T(128)}, /*index=5*/s32[]{:T(128)}) while((s32[]{:T(128)}, f32[2,128,128]{2,1,0:T(8,128)S(1)}, s32[]{:T(128)}, f32[32,2,128,128]{3,2,1,0:T(8,128)}, s32[]{:T(128)}, /*index=5*/s32[]{:T(128)}) %tuple.79), condition=%wide.region_1.2_spmd.clone, body=%wide.region_0.1_spmd.clone.sunk | while | flops 98308 | bytes 393317 | solution.py:30
  102.2 0.9 add_select_fusion.4
  103.2 0.9 add_select_fusion.4
  104.1 0.9 add_select_fusion.4
  105.1 0.9 add_select_fusion.4
  106.1 0.9 add_select_fusion.4
  107.1 0.9 add_select_fusion.4
  108.0 0.9 add_select_fusion.4
  109.0 0.9 add_select_fusion.4
  110.0 0.9 add_select_fusion.4
  110.9 0.9 add_select_fusion.4
  111.9 0.9 add_select_fusion.4
  112.9 0.9 add_select_fusion.4
  113.9 0.9 add_select_fusion.4
  114.8 0.9 add_select_fusion.4
  115.8 0.9 add_select_fusion.4
  116.8 0.9 add_select_fusion.4
  117.8 0.9 add_select_fusion.4
  118.7 0.9 add_select_fusion.4
  119.7 0.9 add_select_fusion.4
  120.7 0.9 add_select_fusion.4
  121.6 0.9 add_select_fusion.4
  122.6 1.0 add_select_fusion.4
  123.6 0.9 add_select_fusion.4
  124.6 0.9 add_select_fusion.4
  125.6 1.0 add_select_fusion.4
  126.6 0.9 add_select_fusion.4
  127.5 0.9 add_select_fusion.4
  128.5 0.9 add_select_fusion.4
  129.5 0.9 add_select_fusion.4
  130.4 0.9 add_select_fusion.4
  132.2 38.9 %all-gather.6.cloned.1.call-done = bf16[256,4096]{1,0:T(8,128)(2,1)} async-done(((bf16[256,128]{1,0:T(8,128)(2,1)}), bf16[256,4096]{1,0:T(8,128)(2,1)}) %all-gather.6.cloned.1.call-update) | async-done | bytes 2097168 | tf_op jit(solution)/shard_map/all_gather | solution.py:44
  171.1 2.3 multiply_reduce_fusion
  174.7 1.1 convolution_select_fusion
  177.4 64.4 %all-gather.10.cloned.1.call-done = f32[64,128,128]{2,1,0:T(8,128)} async-done(((f32[2,128,128]{2,1,0:T(8,128)}), f32[64,128,128]{2,1,0:T(8,128)}) %all-gather.10.cloned.1.call-update) | async-done | bytes 4194320 | tf_op jit(solution)/shard_map/all_gather | solution.py:20
  241.8 4.6 %rev.3 = f32[32,2,128,128]{3,2,1,0:T(8,128)} reverse(f32[32,2,128,128]{3,2,1,0:T(8,128)} %bitcast.117), dimensions={0} | reverse | bytes 8388608 | tf_op jit(solution)/shard_map/rev | solution.py:22
  246.4 30.2 %while.29 = (s32[]{:T(128)}, f32[2,128,128]{2,1,0:T(8,128)S(1)}, s32[]{:T(128)}, f32[32,2,128,128]{3,2,1,0:T(8,128)}, s32[]{:T(128)}, /*index=5*/s32[]{:T(128)}) while((s32[]{:T(128)}, f32[2,128,128]{2,1,0:T(8,128)S(1)}, s32[]{:T(128)}, f32[32,2,128,128]{3,2,1,0:T(8,128)}, s32[]{:T(128)}, /*index=5*/s32[]{:T(128)}) %tuple.70), condition=%wide.region_5.6_spmd.clone, body=%wide.region_4.5_spmd.clone.sunk | while | flops 98308 | bytes 393317 | solution.py:30
  247.4 0.9 add_select_fusion.5
  248.4 0.9 add_select_fusion.5
  249.4 0.9 add_select_fusion.5
  250.3 0.9 add_select_fusion.5
  (63 shorter events, 35.2 us)
Async XLA Ops:
  7.2 1.1 copy-start
  7.2 94.0 %all-gather.8.cloned.1.call-start = ((), (), s32[]{:S(2)}) async-start(), calls=%async_computation.2 | async-start | bytes 4325376 | tf_op jit(solution)/shard_map/all_gather | solution.py:20
  11.6 11.8 %copy-start.1 = (bf16[256,256]{1,0:T(8,128)(2,1)S(1)}, bf16[256,256]{1,0:T(8,128)(2,1)}, u32[]{:S(2)}) copy-start(bf16[256,256]{1,0:T(8,128)(2,1)} %param.9) | copy-start | bytes 393220
  11.6 11.8 %copy-start.2 = (bf16[256,256]{1,0:T(8,128)(2,1)S(1)}, bf16[256,256]{1,0:T(8,128)(2,1)}, u32[]{:S(2)}) copy-start(bf16[256,256]{1,0:T(8,128)(2,1)} %param.10) | copy-start | bytes 393220
  11.6 76.0 %all-to-all-start = ((bf16[16,256,256]{2,1,0:T(8,128)(2,1)}), bf16[16,256,256]{2,1,0:T(8,128)(2,1)S(1)}, u32[]{:S(2)}, u32[]{:S(2)}) async-start(bf16[16,256,256]{2,1,0:T(8,128)(2,1)} %stack.2), calls=%async_computation | async-start | bytes 4194304 | tf_op jit(solution)/shard_map/all_to_all | solution.py:13
  21.9 149.1 %all-gather.6.cloned.1.call-start = ((), (), s32[]{:S(2)}) async-start(), calls=%async_computation.1 | async-start | bytes 2162688 | tf_op jit(solution)/shard_map/all_gather | solution.py:44
  22.7 219.1 %all-gather.10.cloned.1.call-start = ((), (), s32[]{:S(2)}) async-start(), calls=%async_computation.3 | async-start | bytes 4325376 | tf_op jit(solution)/shard_map/all_gather | solution.py:20
  22.8 0.6 copy-start.3
Sparse Core Ops, SparseCore 0:
  10.7 90.4 all-gather.7
  103.3 67.7 all-gather.5
  174.6 67.2 all-gather.9
